TPU v7x, 32 devices: a whole 2x2x4 slice. The times are simulated.
32 devices in a mesh: groups: 2 (over x), tm: 16 (over z, y, core).
Axes of the slice: x: 2, y: 2, z: 4, core: 2. Of those that a mesh axis runs over, the one named last changes fastest.
Arguments:
- observed: float32 [32, 128], P(('groups', 'tm')), parts along dimension 0, may hold values from -6 to 6
- obs_masks: int32 [32, 128], P(('groups', 'tm')), parts along dimension 0, may hold values 0 or 1
- decay_rates: float32 [256], P('groups'), parts along dimension 0, may hold values from 0.05 to 0.5
- noise_var: float32 [256], P('groups'), parts along dimension 0, may hold values from 0.05 to 0.5
- spatial_cov: float32 [256, 128], P('groups'), parts along dimension 0, may hold values from -1 to 4, as said below
Outputs:
- smooth_mean: float32 [32, 256], P(('groups', 'tm')), parts along dimension 0
- smooth_cov: float32 [32, 256, 256], P(('groups', 'tm')), parts along dimension 0
There are 2 independent parts, one for each index of `groups`. A program takes and returns all parts, laid end to end along the dimension named above; each array names one. Nothing has to cross between parts.
Inputs may be any that keep to these rules, and one draw needn't show every extreme that they name: spatial_cov is symmetric, and each diagonal entry is positive and larger than the sum of the magnitudes of the other entries of its row.
All inputs are finite; a program needn't handle non-finite values. No bound on the sum of `obs_masks` on one device may be relied on, other than what follows from the above.
Results may differ from a plain program's by a relative error of at most 0.0003.
Values sent between devices are 32-bit elements; how exact they have to be, the bound alone decides.
No kernel may reach another device: no remote copies, remote signals or barrier semaphores. Data moves between devices by JAX's collectives and lax.ppermute only.
A program may use at most 128 MiB of HBM per device.

v0:
```python
import jax
import jax.numpy as jnp
from jax import lax
from jax.sharding import PartitionSpec as P

HIGHEST = lax.Precision.HIGHEST
JITTER = 0.001


def matmul_hi(left, right):
    return jnp.matmul(left, right, precision=HIGHEST)


def swap_last(matrix):
    return jnp.swapaxes(matrix, -1, -2)


def apply_trans(transit, matrix):
    points = transit.shape[1]
    upper_half = matrix[..., :points, :]
    lower_half = matrix[..., points:, :]
    return jnp.concatenate(
        [
            transit[0][:, None] * upper_half + transit[1][:, None] * lower_half,
            transit[2][:, None] * upper_half + transit[3][:, None] * lower_half,
        ],
        axis=-2,
    )


def build_model(decay_rates, spatial_cov):
    decay_one = jnp.exp(-decay_rates)
    transit = jnp.stack(
        [
            decay_one * (1.0 + decay_rates),
            decay_one * decay_rates,
            -decay_one * decay_rates,
            decay_one * (1.0 - decay_rates),
        ]
    )
    decay_two = jnp.exp(-2.0 * decay_rates)
    var_ff = 1.0 - decay_two * (1.0 + 2.0 * decay_rates + 2.0 * decay_rates * decay_rates)
    cov_fg = 2.0 * decay_rates * decay_rates * decay_two
    var_gg = 1.0 - decay_two * (1.0 - 2.0 * decay_rates + 2.0 * decay_rates * decay_rates)
    fac_ff = jnp.sqrt(var_ff)
    fac_gf = cov_fg / fac_ff
    fac_gg = jnp.sqrt(var_gg - fac_gf * fac_gf)

    def scaled(left, right):
        return left[:, None] * spatial_cov * right[None, :]

    zero_block = jnp.zeros_like(spatial_cov)
    process = jnp.block(
        [
            [scaled(fac_ff, fac_ff), scaled(fac_ff, fac_gf)],
            [scaled(fac_gf, fac_ff), scaled(fac_gf, fac_gf) + scaled(fac_gg, fac_gg)],
        ]
    )
    process = process + JITTER * jnp.eye(2 * spatial_cov.shape[0], dtype=jnp.float32)
    prior = jnp.block([[spatial_cov, zero_block], [zero_block, spatial_cov]])
    return (transit, process, prior)


def predict(transit, process, mean, cov):
    forward_cov = apply_trans(transit, cov)
    cov_pred = apply_trans(transit, swap_last(forward_cov)) + process
    mean_pred = apply_trans(transit, mean[:, None])[:, 0]
    return (mean_pred, cov_pred)


def kalman_update(mean_pred, cov_pred, obs, root):
    points = obs.shape[-1]
    normal = (
        jnp.eye(points, dtype=jnp.float32)
        + root[:, None] * cov_pred[:points, :points] * root[None, :]
    )
    factor = jnp.linalg.cholesky(normal)
    innovation = root * (obs - mean_pred[:points])
    rhs = jnp.concatenate([root[:, None] * cov_pred[:points, :], innovation[:, None]], axis=1)
    half = lax.linalg.triangular_solve(factor, rhs, left_side=True, lower=True)
    gain_half = half[:, :-1]
    cov_new = cov_pred - matmul_hi(swap_last(gain_half), gain_half)
    mean_new = mean_pred + matmul_hi(swap_last(gain_half), half[:, -1])
    return (mean_new, cov_new)


def smoother_elements(means, covs, last_flag, transit, process):
    forward_cov = apply_trans(transit, covs)
    predicted = apply_trans(transit, swap_last(forward_cov)) + process
    factor = jnp.linalg.cholesky(predicted)
    half_solve = lax.linalg.triangular_solve(factor, forward_cov, left_side=True, lower=True)
    gain_t = lax.linalg.triangular_solve(
        factor, half_solve, left_side=True, lower=True, transpose_a=True
    )
    gains = swap_last(gain_t) * (1.0 - last_flag.astype(jnp.float32))[:, None, None]
    forward_mean = apply_trans(transit, means[..., None])
    shift_means = means - matmul_hi(gains, forward_mean)[..., 0]
    shift_covs = covs - matmul_hi(gains, forward_cov)
    return (gains, shift_means, shift_covs)


def smooth_join(lower_el, higher_el):
    gain_a, mean_a, cov_a = lower_el
    gain_b, mean_b, cov_b = higher_el
    return (
        matmul_hi(gain_a, gain_b),
        matmul_hi(gain_a, mean_b[..., None])[..., 0] + mean_a,
        matmul_hi(matmul_hi(gain_a, cov_b), swap_last(gain_a)) + cov_a,
    )


def shards(observed, obs_masks, decay_rates, noise_var, spatial_cov):
    transit, process, prior = build_model(decay_rates, spatial_cov)
    local_steps, points = observed.shape
    width = 2 * points
    position = lax.axis_index("tm")
    tm_count = lax.axis_size("tm")
    total_steps = tm_count * local_steps
    root_local = jnp.sqrt(obs_masks.astype(jnp.float32) / noise_var)
    packed = jnp.stack([observed, root_local], axis=1)
    gathered = lax.all_gather(packed, "tm", tiled=True)
    obs_all = gathered[:, 0]
    root_all = gathered[:, 1]
    mean_first, cov_first = kalman_update(
        jnp.zeros((width,), jnp.float32), prior, obs_all[0], root_all[0]
    )
    last_local = position * local_steps + (local_steps - 1)

    def filter_step(step, mean, cov):
        mean_pred, cov_pred = predict(transit, process, mean, cov)
        obs_now = lax.dynamic_index_in_dim(obs_all, step, keepdims=False)
        root_now = lax.dynamic_index_in_dim(root_all, step, keepdims=False)
        return kalman_update(mean_pred, cov_pred, obs_now, root_now)

    if local_steps == 1:

        def body(step, carry):
            return filter_step(step, carry[0], carry[1])

        mean_last, cov_last = lax.fori_loop(1, last_local + 1, body, (mean_first, cov_first))
        means = mean_last[None]
        covs = cov_last[None]
    else:
        mean_buf = jnp.zeros((local_steps, width), jnp.float32).at[0].set(mean_first)
        cov_buf = jnp.zeros((local_steps, width, width), jnp.float32).at[0].set(cov_first)

        def body(step, carry):
            mean, cov, mean_buf, cov_buf = carry
            mean, cov = filter_step(step, mean, cov)
            slot = step % local_steps
            mean_buf = lax.dynamic_update_index_in_dim(mean_buf, mean, slot, 0)
            cov_buf = lax.dynamic_update_index_in_dim(cov_buf, cov, slot, 0)
            return (mean, cov, mean_buf, cov_buf)

        _, _, means, covs = lax.fori_loop(
            1, last_local + 1, body, (mean_first, cov_first, mean_buf, cov_buf)
        )
    global_step = position * local_steps + jnp.arange(local_steps)
    last_flag = global_step == total_steps - 1
    if local_steps == 1:

        def compute_elements(operand):
            return smoother_elements(operand[0], operand[1], last_flag, transit, process)

        def final_elements(operand):
            return (jnp.zeros_like(operand[1]), operand[0], operand[1])

        smooth = lax.cond(position == tm_count - 1, final_elements, compute_elements, (means, covs))
    else:
        smooth = smoother_elements(means, covs, last_flag, transit, process)
    if local_steps > 1:
        last_el = jax.tree.map(lambda leaf: leaf[-1], smooth)
        front_els = jax.tree.map(lambda leaf: leaf[:-1], smooth)

        def backward(running, element):
            joined = smooth_join(element, running)
            return (joined, joined)

        _, head_els = lax.scan(backward, last_el, front_els, reverse=True)
        suffixes = jax.tree.map(
            lambda head_leaf, last_leaf: jnp.concatenate([head_leaf, last_leaf[None]], axis=0),
            head_els,
            last_el,
        )
        block_total = jax.tree.map(lambda leaf: leaf[0], suffixes)
    else:
        block_total = jax.tree.map(lambda leaf: leaf[0], smooth)
    running = block_total
    shift = 1
    while shift < tm_count:
        pairs = [(source, source - shift) for source in range(shift, tm_count)]
        received = lax.ppermute(running, "tm", pairs)
        running = smooth_join(running, received)
        shift *= 2
    if local_steps == 1:
        return (running[1][None], running[2][None])
    pairs = [(source, source - 1) for source in range(1, tm_count)]
    after_mine = lax.ppermute(running, "tm", pairs)
    gains, shift_means, shift_covs = suffixes
    smooth_mean = matmul_hi(gains, after_mine[1][:, None])[..., 0] + shift_means
    smooth_cov = matmul_hi(matmul_hi(gains, after_mine[2]), swap_last(gains)) + shift_covs
    return (smooth_mean, smooth_cov)


def solution(mesh):
    placed = (
        P(("groups", "tm"), None),
        P(("groups", "tm"), None),
        P("groups"),
        P("groups"),
        P("groups", None),
    )
    return jax.shard_map(
        shards,
        mesh=mesh,
        in_specs=placed,
        out_specs=(P(("groups", "tm"), None), P(("groups", "tm"), None, None)),
        check_vma=False,
    )
```

profile of v0, /device:TPU:1, one launch (start us, length us, event | category | flops | bytes accessed | tf_op | source)
XLA Modules:
  0.0 498.3 jit_solution(2744481612989866936)
XLA Ops:
  0.7 0.6 copy-done.3
  1.3 0.7 copy-done.1
  2.0 23.1 %all_gather.3 = f32[16,2,128]{2,1,0:T(2,128)S(1)} all-gather(f32[1,2,128]{2,1,0:T(2,128)S(1)} %pad_maximum_fusion.3), channel_id=1, replica_groups=mesh['groups'=2,'tm'=16] {'tm'}, dimensions={0}, use_global_device_ids=true | all-gather | bytes 17408 | tf_op jit(solution)/shard_map/all_gather | solution.py:121
  25.7 11.7 %custom-call.32 = f32[128,128]{1,0:T(8,128)S(1)} custom-call(f32[128,128]{1,0:T(8,128)S(1)} %fusion.49), custom_call_target="Cholesky" | custom-call | tf_op jit(solution)/shard_map/jit(cholesky)/cholesky/custom-call.1 | solution.py:77
  37.5 0.7 compare_reduce_fusion.3
  38.2 0.6 fusion.47
  38.8 9.8 %custom-call.33 = f32[1,128,128]{1,2,0:T(8,128)S(1)} custom-call(f32[1,128,128]{2,1,0:T(8,128)S(1)} %fusion.47), custom_call_target="InvertDiagBlocksLowerTriangular" | custom-call | tf_op jit(solution)/shard_map/triangular_solve/custom-call.0 | solution.py:80
  49.9 24.9 %while.14 = (s32[]{:T(128)}, f32[256]{0:T(256)S(1)}, f32[256,256]{0,1:T(8,128)S(1)}, s32[]{:T(128)}, f32[128]{0:T(128)S(1)}, /*index=5*/f32[128]{0:T(128)S(1)}, ...) while((s32[]{:T(128)}, f32[256]{0:T(256)S(1)}, ...), condition=%wide.region_3.6_spmd, body=%wide.region_2.5_spmd.sunk | while | flops 152618752 | bytes 5461689 | solution.py:140
  51.0 11.7 %custom-call.37 = f32[128,128]{1,0:T(8,128)S(1)} custom-call(f32[128,128]{1,0:T(8,128)S(1)} %fusion.129), custom_call_target="Cholesky" | custom-call | tf_op jit(solution)/shard_map/while/body/jit(cholesky)/cholesky/custom-call.1 | solution.py:77
  62.7 0.7 compare_reduce_fusion.5
  63.4 0.6 fusion.130
  64.0 9.8 %custom-call.38 = f32[1,128,128]{1,2,0:T(8,128)S(1)} custom-call(f32[1,128,128]{2,1,0:T(8,128)S(1)} %fusion.130), custom_call_target="InvertDiagBlocksLowerTriangular" | custom-call | tf_op jit(solution)/shard_map/while/body/triangular_solve/custom-call.0 | solution.py:80
  74.9 63.7 %conditional.1 = (f32[1,256]{1,0:T(1,128)S(1)}, f32[256,256]{0,1:T(8,128)S(1)}, f32[1,256,256]{2,1,0:T(8,128)S(1)}) conditional(s32[]{:T(128)} %convert_element_type.18, (f32[128]{0:T(128)S(1)}, f32[1,256,256]{1,2,0:T(8,128)S(1)}, f32[128]{0:T(128)S(1)}, f32[128]{0:T(128)S(1)}, f32[128]{0:T(128)S(1)}, /*index=5*/f32[256,256]{0,1:T(8,128)S(1)}, ...), branch_computations={%region_4.11_spmd, %region_9.12_spmd} | conditional | flops 556025344 | bytes 11482373 | solution.py:168
  76.0 11.7 %custom-call.24 = f32[1,128,128]{2,1,0:T(8,128)S(1)} custom-call(f32[1,128,128]{2,1,0:T(8,128)S(1)} %cholesky.48), custom_call_target="Cholesky" | custom-call | tf_op jit(solution)/shard_map/cond/branch_0_fun/jit(cholesky)/cholesky | solution.py:90
  87.7 9.8 %custom-call.25 = f32[1,1,128,128]{2,3,1,0:T(8,128)S(1)} custom-call(f32[1,1,128,128]{3,2,1,0:T(8,128)S(1)} %get-tuple-element.221), custom_call_target="InvertDiagBlocksLowerTriangular" | custom-call | tf_op jit(solution)/shard_map/cond/branch_0_fun/jit(cholesky)/cholesky | solution.py:90
  98.0 11.7 %custom-call.26 = f32[1,128,128]{2,1,0:T(8,128)S(1)} custom-call(f32[1,128,128]{2,1,0:T(8,128)S(1)} %fusion.20), custom_call_target="Cholesky" | custom-call | tf_op jit(solution)/shard_map/cond/branch_0_fun/jit(cholesky)/cholesky | solution.py:90
  109.8 0.7 compare_reduce_fusion.1
  111.8 4.0 while.13
  111.9 0.6 fusion.133
  112.5 1.3 bitcast_dynamic-update-slice_fusion.3
  113.8 0.6 fusion.133
  114.4 1.3 bitcast_dynamic-update-slice_fusion.3
  115.7 19.7 %custom-call.27 = f32[1,2,128,128]{2,3,1,0:T(8,128)S(1)} custom-call(f32[1,2,128,128]{3,2,1,0:T(8,128)S(1)} %bitcast.262), custom_call_target="InvertDiagBlocksLowerTriangular" | custom-call | tf_op jit(solution)/shard_map/cond/branch_0_fun/triangular_solve | solution.py:92
  137.7 0.6 fusion.17
  138.6 1.9 collective-permute-start.7
  140.5 1.9 collective-permute-start.3
  142.4 1.9 collective-permute-start
  144.3 22.5 %collective-permute-done.3 = f32[256]{0:T(256)S(1)} collective-permute-done((f32[256]{0:T(256)S(1)}, f32[256]{0:T(256)S(1)}, u32[]{:S(2)}, u32[]{:S(2)}) %collective-permute-start.3) | collective-permute-done | bytes 1056 | tf_op jit(solution)/shard_map/ppermute | solution.py:192
  167.0 1.3 collective-permute-start.4
  168.4 0.6 fusion.65
  169.4 1.3 collective-permute-start.8
  170.7 0.6 fusion.59
  171.3 1.3 collective-permute-start.1
  172.6 48.7 %collective-permute-done.4 = f32[256]{0:T(256)S(1)} collective-permute-done((f32[256]{0:T(256)S(1)}, f32[256]{0:T(256)S(1)}, u32[]{:S(2)}, u32[]{:S(2)}) %collective-permute-start.4) | collective-permute-done | bytes 1056 | tf_op jit(solution)/shard_map/ppermute | solution.py:192
  221.6 1.3 collective-permute-start.5
  222.9 4.1 collective-permute-done.8
  227.8 1.3 collective-permute-start.9
  229.1 0.7 collective-permute-done.1
  230.2 1.3 collective-permute-start.2
  231.5 89.9 %collective-permute-done.5 = f32[256]{0:T(256)S(1)} collective-permute-done((f32[256]{0:T(256)S(1)}, f32[256]{0:T(256)S(1)}, u32[]{:S(2)}, u32[]{:S(2)}) %collective-permute-start.5) | collective-permute-done | bytes 1056 | tf_op jit(solution)/shard_map/ppermute | solution.py:192
  321.7 1.3 collective-permute-start.6
  323.1 7.4 %collective-permute-done.9 = f32[256,256]{1,0:T(8,128)S(1)} collective-permute-done((f32[256,256]{1,0:T(8,128)S(1)}, f32[256,256]{1,0:T(8,128)S(1)}, u32[]{:S(2)}, u32[]{:S(2)}) %collective-permute-start.9) | collective-permute-done | bytes 262176 | tf_op jit(solution)/shard_map/ppermute | solution.py:192
  331.3 1.3 collective-permute-start.10
  332.6 0.7 collective-permute-done.2
  333.7 145.0 %collective-permute-done.6 = f32[256]{0:T(256)S(1)} collective-permute-done((f32[256]{0:T(256)S(1)}, f32[256]{0:T(256)S(1)}, u32[]{:S(2)}, u32[]{:S(2)}) %collective-permute-start.6) | collective-permute-done | bytes 1056 | tf_op jit(solution)/shard_map/ppermute | solution.py:192
  478.7 0.9 convolution_add_fusion.4
  479.6 17.0 %collective-permute-done.10 = f32[256,256]{1,0:T(8,128)S(1)} collective-permute-done((f32[256,256]{1,0:T(8,128)S(1)}, f32[256,256]{1,0:T(8,128)S(1)}, u32[]{:S(2)}, u32[]{:S(2)}) %collective-permute-start.10) | collective-permute-done | bytes 262176 | tf_op jit(solution)/shard_map/ppermute | solution.py:192
  496.9 1.1 fusion.38
  (91 shorter events, 10.8 us)
Async XLA Ops:
  0.6 0.7 copy-start.3
  0.6 0.7 copy-start.4
  1.3 0.7 copy-start.1
  2.0 23.2 %copy-start.2 = (f32[128]{0:T(128)S(1)}, f32[128]{0:T(128)}, u32[]{:S(2)}) copy-start(f32[128]{0:T(128)} %param.14) | copy-start | bytes 1540
  2.0 23.3 %copy-start = (f32[128,128]{1,0:T(8,128)S(1)}, f32[128,128]{1,0:T(8,128)}, u32[]{:S(2)}) copy-start(f32[128,128]{1,0:T(8,128)} %param.16) | copy-start | bytes 196612
  138.6 29.8 %collective-permute-start.7 = (f32[256,256]{1,0:T(8,128)S(1)}, f32[256,256]{1,0:T(8,128)S(1)}, u32[]{:S(2)}, u32[]{:S(2)}) collective-permute-start(f32[256,256]{1,0:T(8,128)S(1)} %bitcast.242), channel_id=1, source_target_pairs={{1,0},{2,1},{3,2},{4,3},{5,4},{6,5},{7,6},{8,7},{9,8},{10,9},{11,1... | collective-permute-start | bytes 786440 | tf_op jit(solution)/shard_map/ppermute | solution.py:192
  140.5 26.3 %collective-permute-start.3 = (f32[256]{0:T(256)S(1)}, f32[256]{0:T(256)S(1)}, u32[]{:S(2)}, u32[]{:S(2)}) collective-permute-start(f32[256]{0:T(256)S(1)} %bitcast.255), channel_id=1, source_target_pairs={{1,0},{2,1},{3,2},{4,3},{5,4},{6,5},{7,6},{8,7},{9,8},{10,9},{11,1... | collective-permute-start | bytes 3080 | tf_op jit(solution)/shard_map/ppermute | solution.py:192
  142.4 28.2 %collective-permute-start = (f32[256,256]{0,1:T(8,128)S(1)}, f32[256,256]{0,1:T(8,128)S(1)}, u32[]{:S(2)}, u32[]{:S(2)}) collective-permute-start(f32[256,256]{0,1:T(8,128)S(1)} %get-tuple-element.136), channel_id=1, source_target_pairs={{1,0},{2,1},{3,2},{4,3},{5,4},{6,5},{7,6},{8,7},{9,8},{10,9},{11,1... | collective-permute-start | bytes 786440 | tf_op jit(solution)/shard_map/ppermute | solution.py:192
  167.0 54.3 %collective-permute-start.4 = (f32[256]{0:T(256)S(1)}, f32[256]{0:T(256)S(1)}, u32[]{:S(2)}, u32[]{:S(2)}) collective-permute-start(f32[256]{0:T(256)S(1)} %add.183), channel_id=1, source_target_pairs={{2,0},{3,1},{4,2},{5,3},{6,4},{7,5},{8,6},{9,7},{10,8},{11,9},{12,... | collective-permute-start | bytes 3080 | tf_op jit(solution)/shard_map/ppermute | solution.py:192
  169.4 57.7 %collective-permute-start.8 = (f32[256,256]{1,0:T(8,128)S(1)}, f32[256,256]{1,0:T(8,128)S(1)}, u32[]{:S(2)}, u32[]{:S(2)}) collective-permute-start(f32[256,256]{1,0:T(8,128)S(1)} %convolution_add_fusion.3), channel_id=1, source_target_pairs={{2,0},{3,1},{4,2},{5,3},{6,4},{7,5},{8,6},{9,7},{10,8},{11,9},{12,... | collective-permute-start | bytes 786440 | tf_op jit(solution)/shard_map/ppermute | solution.py:192
  171.3 58.6 %collective-permute-start.1 = (f32[256,256]{1,0:T(8,128)S(1)}, f32[256,256]{1,0:T(8,128)S(1)}, u32[]{:S(2)}, u32[]{:S(2)}) collective-permute-start(f32[256,256]{1,0:T(8,128)S(1)} %fusion.59), channel_id=1, source_target_pairs={{2,0},{3,1},{4,2},{5,3},{6,4},{7,5},{8,6},{9,7},{10,8},{11,9},{12,... | collective-permute-start | bytes 786440 | tf_op jit(solution)/shard_map/ppermute | solution.py:192
  221.6 99.9 %collective-permute-start.5 = (f32[256]{0:T(256)S(1)}, f32[256]{0:T(256)S(1)}, u32[]{:S(2)}, u32[]{:S(2)}) collective-permute-start(f32[256]{0:T(256)S(1)} %add.184), channel_id=1, source_target_pairs={{4,0},{5,1},{6,2},{7,3},{8,4},{9,5},{10,6},{11,7},{12,8},{13,9},{1... | collective-permute-start | bytes 3080 | tf_op jit(solution)/shard_map/ppermute | solution.py:192
  227.8 102.6 %collective-permute-start.9 = (f32[256,256]{1,0:T(8,128)S(1)}, f32[256,256]{1,0:T(8,128)S(1)}, u32[]{:S(2)}, u32[]{:S(2)}) collective-permute-start(f32[256,256]{1,0:T(8,128)S(1)} %convolution_add_fusion.2), channel_id=1, source_target_pairs={{4,0},{5,1},{6,2},{7,3},{8,4},{9,5},{10,6},{11,7},{12,8},{13,9},{1... | collective-permute-start | bytes 786440 | tf_op jit(solution)/shard_map/ppermute | solution.py:192
  230.2 103.1 %collective-permute-start.2 = (f32[256,256]{1,0:T(8,128)S(1)}, f32[256,256]{1,0:T(8,128)S(1)}, u32[]{:S(2)}, u32[]{:S(2)}) collective-permute-start(f32[256,256]{1,0:T(8,128)S(1)} %fusion.60), channel_id=1, source_target_pairs={{4,0},{5,1},{6,2},{7,3},{8,4},{9,5},{10,6},{11,7},{12,8},{13,9},{1... | collective-permute-start | bytes 786440 | tf_op jit(solution)/shard_map/ppermute | solution.py:192
  321.7 156.9 %collective-permute-start.6 = (f32[256]{0:T(256)S(1)}, f32[256]{0:T(256)S(1)}, u32[]{:S(2)}, u32[]{:S(2)}) collective-permute-start(f32[256]{0:T(256)S(1)} %add.185), channel_id=1, source_target_pairs={{8,0},{9,1},{10,2},{11,3},{12,4},{13,5},{14,6},{15,7},{24,16},{25,... | collective-permute-start | bytes 3080 | tf_op jit(solution)/shard_map/ppermute | solution.py:192
  331.3 165.3 %collective-permute-start.10 = (f32[256,256]{1,0:T(8,128)S(1)}, f32[256,256]{1,0:T(8,128)S(1)}, u32[]{:S(2)}, u32[]{:S(2)}) collective-permute-start(f32[256,256]{1,0:T(8,128)S(1)} %convolution_add_fusion.1), channel_id=1, source_target_pairs={{8,0},{9,1},{10,2},{11,3},{12,4},{13,5},{14,6},{15,7},{24,16},{25,... | collective-permute-start | bytes 786440 | tf_op jit(solution)/shard_map/ppermute | solution.py:192
where the time goes:
time: 505 us; the launch traced here: 498 us
  waiting for transfers between devices  336 us (67%)
  other arithmetic  100 us (20%)
  blocking collectives  23.1 us (5%)
  starting transfers between devices  16.2 us (3%)
  matrix products  12.2 us (2%)
  local copies, waits for them, and re-layouts  6.42 us (1%)
    ppermute x11, waiting for transfers between devices, shards(): received = lax.ppermute(running, 'tm', pairs)  336 us
    another operation x6, other arithmetic, smoother_elements(): factor = jnp.linalg.cholesky(predicted)  34 us
    another operation x6, other arithmetic, kalman_update(): factor = jnp.linalg.cholesky(normal)  24.9 us
    all_gather x1, blocking collectives, shards(): gathered = lax.all_gather(packed, 'tm', tiled=True)  23.1 us
    another operation x4, other arithmetic, kalman_update(): half = lax.linalg.triangular_solve(factor, rhs, left_side=True, lower=True)  20.9 us
    another operation x3, other arithmetic, smoother_elements(): lax.linalg.triangular_solve(factor, half_solve, left_side=True, lower=Tru...  19.7 us
    ppermute x11, starting transfers between devices, shards(): received = lax.ppermute(running, 'tm', pairs)  16.2 us
  transfers between devices with their start and end apart: 11, of which 9 were waited for; matrix products, arithmetic and copies ran while one was open for 1% of the time, Pallas kernels for 0%

commit v1 on v0

--- a/solution.py
+++ b/solution.py
@@ -118,7 +118,14 @@
     total_steps = tm_count * local_steps
     root_local = jnp.sqrt(obs_masks.astype(jnp.float32) / noise_var)
     packed = jnp.stack([observed, root_local], axis=1)
-    gathered = lax.all_gather(packed, "tm", tiled=True)
+    ways, here, lap = (lax.axis_size("tm"), lax.axis_index("tm"), packed.shape[0])
+    line, have = (packed, 1)
+    while have < ways:
+        line = jnp.concatenate(
+            [line, lax.ppermute(line, "tm", [(d, (d - have) % ways) for d in range(ways)])], axis=0
+        )
+        have = 2 * have
+    gathered = jnp.roll(line, here * lap, axis=0)
     obs_all = gathered[:, 0]
     root_all = gathered[:, 1]
     mean_first, cov_first = kalman_update(

time: 505 us -> 506 us (level)
  blocking collectives: 23.1 us -> 0 us
  waiting for transfers between devices: 336 us -> 350 us
  starting transfers between devices: 16.2 us -> 23.9 us
    all_gather x1 -> x0, blocking collectives: 23.1 us -> none  [shards(): gathered = lax.all_gather(packed, 'tm', tiled=True)]
    ppermute x0 -> x4, waiting for transfers between devices: none -> 8.26 us  [shards(): lax.ppermute(line, 'tm', [(d, (d - have) % ways) for d in range(ways)])]
    ppermute x0 -> x4, starting transfers between devices: none -> 7.66 us  [shards(): lax.ppermute(line, 'tm', [(d, (d - have) % ways) for d in range(ways)])]
    ppermute x11, waiting for transfers between devices: 336 us -> 342 us  [shards(): received = lax.ppermute(running, 'tm', pairs)]
  transfers between devices with their start and end apart: 11 -> 15, of which waited for: 9 -> 13; matrix products, arithmetic and copies ran while one was open for 1% -> 1% of each run, Pallas kernels for 0% -> 0%
where the time goes in v1:
time: 506 us; the launch traced here: 499 us
  waiting for transfers between devices  350 us (69%)
  other arithmetic  101 us (20%)
  starting transfers between devices  23.9 us (5%)
  matrix products  12.2 us (2%)
  local copies, waits for them, and re-layouts  8.22 us (2%)
    ppermute x11, waiting for transfers between devices, shards(): received = lax.ppermute(running, 'tm', pairs)  342 us
    another operation x6, other arithmetic, smoother_elements(): factor = jnp.linalg.cholesky(predicted)  34 us
    another operation x6, other arithmetic, kalman_update(): factor = jnp.linalg.cholesky(normal)  24.8 us
    another operation x4, other arithmetic, kalman_update(): half = lax.linalg.triangular_solve(factor, rhs, left_side=True, lower=True)  20.8 us
    another operation x3, other arithmetic, smoother_elements(): lax.linalg.triangular_solve(factor, half_solve, left_side=True, lower=Tru...  19.7 us
    ppermute x11, starting transfers between devices, shards(): received = lax.ppermute(running, 'tm', pairs)  16.2 us
  transfers between devices with their start and end apart: 15, of which 13 were waited for; matrix products, arithmetic and copies ran while one was open for 1% of the time, Pallas kernels for 0%

profile of v1, /device:TPU:1, one launch (start us, length us, event | category | flops | bytes accessed | tf_op | source)
XLA Modules:
  0.0 499.2 jit_solution(3551064235634140143)
XLA Ops:
  0.6 0.7 sqrt_bitcast_fusion
  1.3 0.7 copy-done.1
  2.0 0.7 copy-done.2
  2.7 0.9 copy.17
  3.7 2.2 collective-permute-done
  5.9 7.0 %collective-permute-start.1 = (f32[2,2,128]{2,1,0:T(2,128)S(1)}, f32[2,2,128]{2,1,0:T(2,128)S(1)}, u32[]{:S(2)}, u32[]{:S(2)}) collective-permute-start(f32[2,2,128]{2,1,0:T(2,128)S(1)} %pad_maximum_fusion.5), channel_id=1, source_target_pairs={{0,14},{1,15},{2,0},{3,1},{4,2},{5,3},{6,4},{7,5},{8,6},{9,7},{10,... | collective-permute-start | bytes 6152 | tf_op jit(solution)/shard_map/ppermute | solution.py:125
  12.8 0.7 collective-permute-done.1
  14.2 1.9 collective-permute-done.2
  16.2 3.5 collective-permute-done.3
  20.8 11.7 %custom-call.32 = f32[128,128]{1,0:T(8,128)S(1)} custom-call(f32[128,128]{1,0:T(8,128)S(1)} %fusion.49), custom_call_target="Cholesky" | custom-call | tf_op jit(solution)/shard_map/jit(cholesky)/cholesky/custom-call.1 | solution.py:77
  32.6 0.6 compare_reduce_fusion.3
  33.8 9.8 %custom-call.33 = f32[1,128,128]{1,2,0:T(8,128)S(1)} custom-call(f32[1,128,128]{2,1,0:T(8,128)S(1)} %fusion.47), custom_call_target="InvertDiagBlocksLowerTriangular" | custom-call | tf_op jit(solution)/shard_map/triangular_solve/custom-call.0 | solution.py:80
  44.9 24.8 %while.14 = (s32[]{:T(128)}, f32[256]{0:T(256)S(1)}, f32[256,256]{0,1:T(8,128)S(1)}, s32[]{:T(128)}, f32[128]{0:T(128)S(1)}, /*index=5*/f32[128]{0:T(128)S(1)}, ...) while((s32[]{:T(128)}, f32[256]{0:T(256)S(1)}, ...), condition=%wide.region_3.6_spmd, body=%wide.region_2.5_spmd.sunk | while | flops 152618752 | bytes 5461689 | solution.py:147
  45.9 11.7 %custom-call.39 = f32[128,128]{1,0:T(8,128)S(1)} custom-call(f32[128,128]{1,0:T(8,128)S(1)} %fusion.130), custom_call_target="Cholesky" | custom-call | tf_op jit(solution)/shard_map/while/body/jit(cholesky)/cholesky/custom-call.1 | solution.py:77
  58.9 9.8 %custom-call.40 = f32[1,128,128]{1,2,0:T(8,128)S(1)} custom-call(f32[1,128,128]{2,1,0:T(8,128)S(1)} %fusion.131), custom_call_target="InvertDiagBlocksLowerTriangular" | custom-call | tf_op jit(solution)/shard_map/while/body/triangular_solve/custom-call.0 | solution.py:80
  69.7 64.1 %conditional.1 = (f32[1,256]{1,0:T(1,128)S(1)}, f32[256,256]{0,1:T(8,128)S(1)}, f32[1,256,256]{2,1,0:T(8,128)S(1)}) conditional(s32[]{:T(128)} %convert_element_type.18, (f32[128]{0:T(128)S(1)}, f32[1,256,256]{1,2,0:T(8,128)S(1)}, f32[128]{0:T(128)S(1)}, f32[128]{0:T(128)S(1)}, f32[128]{0:T(128)S(1)}, /*index=5*/f32[256,256]{0,1:T(8,128)S(1)}, ...), branch_computations={%region_4.11_spmd, %region_9.12_spmd} | conditional | flops 556025344 | bytes 11482373 | solution.py:175
  70.8 11.7 %custom-call.24 = f32[1,128,128]{2,1,0:T(8,128)S(1)} custom-call(f32[1,128,128]{2,1,0:T(8,128)S(1)} %cholesky.48), custom_call_target="Cholesky" | custom-call | tf_op jit(solution)/shard_map/cond/branch_0_fun/jit(cholesky)/cholesky | solution.py:90
  82.6 9.8 %custom-call.25 = f32[1,1,128,128]{2,3,1,0:T(8,128)S(1)} custom-call(f32[1,1,128,128]{3,2,1,0:T(8,128)S(1)} %get-tuple-element.207), custom_call_target="InvertDiagBlocksLowerTriangular" | custom-call | tf_op jit(solution)/shard_map/cond/branch_0_fun/jit(cholesky)/cholesky | solution.py:90
  92.9 11.7 %custom-call.26 = f32[1,128,128]{2,1,0:T(8,128)S(1)} custom-call(f32[1,128,128]{2,1,0:T(8,128)S(1)} %fusion.20), custom_call_target="Cholesky" | custom-call | tf_op jit(solution)/shard_map/cond/branch_0_fun/jit(cholesky)/cholesky | solution.py:90
  104.7 0.7 compare_reduce_fusion.1
  106.8 4.2 while.13
  106.9 0.7 fusion.134
  107.6 1.3 bitcast_dynamic-update-slice_fusion.3
  109.0 0.7 fusion.134
  109.6 1.3 bitcast_dynamic-update-slice_fusion.3
  111.0 19.7 %custom-call.27 = f32[1,2,128,128]{2,3,1,0:T(8,128)S(1)} custom-call(f32[1,2,128,128]{3,2,1,0:T(8,128)S(1)} %bitcast.266), custom_call_target="InvertDiagBlocksLowerTriangular" | custom-call | tf_op jit(solution)/shard_map/cond/branch_0_fun/triangular_solve | solution.py:92
  133.8 1.9 collective-permute-start.11
  135.7 1.9 collective-permute-start.7
  137.7 1.9 collective-permute-start.4
  139.6 27.3 %collective-permute-done.7 = f32[256]{0:T(256)S(1)} collective-permute-done((f32[256]{0:T(256)S(1)}, f32[256]{0:T(256)S(1)}, u32[]{:S(2)}, u32[]{:S(2)}) %collective-permute-start.7) | collective-permute-done | bytes 1056 | tf_op jit(solution)/shard_map/ppermute | solution.py:199
  167.1 1.3 collective-permute-start.8
  169.4 1.3 collective-permute-start.12
  171.3 1.3 collective-permute-start.5
  172.6 46.0 %collective-permute-done.8 = f32[256]{0:T(256)S(1)} collective-permute-done((f32[256]{0:T(256)S(1)}, f32[256]{0:T(256)S(1)}, u32[]{:S(2)}, u32[]{:S(2)}) %collective-permute-start.8) | collective-permute-done | bytes 1056 | tf_op jit(solution)/shard_map/ppermute | solution.py:199
  219.0 1.3 collective-permute-start.9
  220.3 4.1 collective-permute-done.12
  225.2 1.3 collective-permute-start.13
  226.5 0.7 collective-permute-done.5
  227.6 1.3 collective-permute-start.6
  228.9 91.4 %collective-permute-done.9 = f32[256]{0:T(256)S(1)} collective-permute-done((f32[256]{0:T(256)S(1)}, f32[256]{0:T(256)S(1)}, u32[]{:S(2)}, u32[]{:S(2)}) %collective-permute-start.9) | collective-permute-done | bytes 1056 | tf_op jit(solution)/shard_map/ppermute | solution.py:199
  320.6 1.3 collective-permute-start.10
  322.0 7.4 %collective-permute-done.13 = f32[256,256]{1,0:T(8,128)S(1)} collective-permute-done((f32[256,256]{1,0:T(8,128)S(1)}, f32[256,256]{1,0:T(8,128)S(1)}, u32[]{:S(2)}, u32[]{:S(2)}) %collective-permute-start.13) | collective-permute-done | bytes 262176 | tf_op jit(solution)/shard_map/ppermute | solution.py:199
  330.2 1.3 collective-permute-start.14
  331.5 0.7 collective-permute-done.6
  332.6 147.0 %collective-permute-done.10 = f32[256]{0:T(256)S(1)} collective-permute-done((f32[256]{0:T(256)S(1)}, f32[256]{0:T(256)S(1)}, u32[]{:S(2)}, u32[]{:S(2)}) %collective-permute-start.10) | collective-permute-done | bytes 1056 | tf_op jit(solution)/shard_map/ppermute | solution.py:199
  479.6 0.9 convolution_add_fusion.4
  480.5 17.0 %collective-permute-done.14 = f32[256,256]{1,0:T(8,128)S(1)} collective-permute-done((f32[256,256]{1,0:T(8,128)S(1)}, f32[256,256]{1,0:T(8,128)S(1)}, u32[]{:S(2)}, u32[]{:S(2)}) %collective-permute-start.14) | collective-permute-done | bytes 262176 | tf_op jit(solution)/shard_map/ppermute | solution.py:199
  497.8 1.1 fusion.38
  (106 shorter events, 15.7 us)
Async XLA Ops:
  1.3 0.7 copy-start.1
  2.0 3.9 collective-permute-start
  2.0 0.7 copy-start.2
  5.9 7.7 %collective-permute-start.1 = (f32[2,2,128]{2,1,0:T(2,128)S(1)}, f32[2,2,128]{2,1,0:T(2,128)S(1)}, u32[]{:S(2)}, u32[]{:S(2)}) collective-permute-start(f32[2,2,128]{2,1,0:T(2,128)S(1)} %pad_maximum_fusion.5), channel_id=1, source_target_pairs={{0,14},{1,15},{2,0},{3,1},{4,2},{5,3},{6,4},{7,5},{8,6},{9,7},{10,... | collective-permute-start | bytes 6152 | tf_op jit(solution)/shard_map/ppermute | solution.py:125
  13.6 2.5 collective-permute-start.2
  16.1 3.5 collective-permute-start.3
  19.7 0.8 copy-start
  133.8 34.6 %collective-permute-start.11 = (f32[256,256]{1,0:T(8,128)S(1)}, f32[256,256]{1,0:T(8,128)S(1)}, u32[]{:S(2)}, u32[]{:S(2)}) collective-permute-start(f32[256,256]{1,0:T(8,128)S(1)} %bitcast.242), channel_id=1, source_target_pairs={{1,0},{2,1},{3,2},{4,3},{5,4},{6,5},{7,6},{8,7},{9,8},{10,9},{11,1... | collective-permute-start | bytes 786440 | tf_op jit(solution)/shard_map/ppermute | solution.py:199
  135.7 31.2 %collective-permute-start.7 = (f32[256]{0:T(256)S(1)}, f32[256]{0:T(256)S(1)}, u32[]{:S(2)}, u32[]{:S(2)}) collective-permute-start(f32[256]{0:T(256)S(1)} %bitcast.260), channel_id=1, source_target_pairs={{1,0},{2,1},{3,2},{4,3},{5,4},{6,5},{7,6},{8,7},{9,8},{10,9},{11,1... | collective-permute-start | bytes 3080 | tf_op jit(solution)/shard_map/ppermute | solution.py:199
  137.7 33.1 %collective-permute-start.4 = (f32[256,256]{0,1:T(8,128)S(1)}, f32[256,256]{0,1:T(8,128)S(1)}, u32[]{:S(2)}, u32[]{:S(2)}) collective-permute-start(f32[256,256]{0,1:T(8,128)S(1)} %get-tuple-element.136), channel_id=1, source_target_pairs={{1,0},{2,1},{3,2},{4,3},{5,4},{6,5},{7,6},{8,7},{9,8},{10,9},{11,1... | collective-permute-start | bytes 786440 | tf_op jit(solution)/shard_map/ppermute | solution.py:199
  167.1 51.6 %collective-permute-start.8 = (f32[256]{0:T(256)S(1)}, f32[256]{0:T(256)S(1)}, u32[]{:S(2)}, u32[]{:S(2)}) collective-permute-start(f32[256]{0:T(256)S(1)} %add.195), channel_id=1, source_target_pairs={{2,0},{3,1},{4,2},{5,3},{6,4},{7,5},{8,6},{9,7},{10,8},{11,9},{12,... | collective-permute-start | bytes 3080 | tf_op jit(solution)/shard_map/ppermute | solution.py:199
  169.4 55.0 %collective-permute-start.12 = (f32[256,256]{1,0:T(8,128)S(1)}, f32[256,256]{1,0:T(8,128)S(1)}, u32[]{:S(2)}, u32[]{:S(2)}) collective-permute-start(f32[256,256]{1,0:T(8,128)S(1)} %convolution_add_fusion.3), channel_id=1, source_target_pairs={{2,0},{3,1},{4,2},{5,3},{6,4},{7,5},{8,6},{9,7},{10,8},{11,9},{12,... | collective-permute-start | bytes 786440 | tf_op jit(solution)/shard_map/ppermute | solution.py:199
  171.3 55.9 %collective-permute-start.5 = (f32[256,256]{1,0:T(8,128)S(1)}, f32[256,256]{1,0:T(8,128)S(1)}, u32[]{:S(2)}, u32[]{:S(2)}) collective-permute-start(f32[256,256]{1,0:T(8,128)S(1)} %fusion.60), channel_id=1, source_target_pairs={{2,0},{3,1},{4,2},{5,3},{6,4},{7,5},{8,6},{9,7},{10,8},{11,9},{12,... | collective-permute-start | bytes 786440 | tf_op jit(solution)/shard_map/ppermute | solution.py:199
  219.0 101.4 %collective-permute-start.9 = (f32[256]{0:T(256)S(1)}, f32[256]{0:T(256)S(1)}, u32[]{:S(2)}, u32[]{:S(2)}) collective-permute-start(f32[256]{0:T(256)S(1)} %add.196), channel_id=1, source_target_pairs={{4,0},{5,1},{6,2},{7,3},{8,4},{9,5},{10,6},{11,7},{12,8},{13,9},{1... | collective-permute-start | bytes 3080 | tf_op jit(solution)/shard_map/ppermute | solution.py:199
  225.2 104.1 %collective-permute-start.13 = (f32[256,256]{1,0:T(8,128)S(1)}, f32[256,256]{1,0:T(8,128)S(1)}, u32[]{:S(2)}, u32[]{:S(2)}) collective-permute-start(f32[256,256]{1,0:T(8,128)S(1)} %convolution_add_fusion.2), channel_id=1, source_target_pairs={{4,0},{5,1},{6,2},{7,3},{8,4},{9,5},{10,6},{11,7},{12,8},{13,9},{1... | collective-permute-start | bytes 786440 | tf_op jit(solution)/shard_map/ppermute | solution.py:199
  227.6 104.6 %collective-permute-start.6 = (f32[256,256]{1,0:T(8,128)S(1)}, f32[256,256]{1,0:T(8,128)S(1)}, u32[]{:S(2)}, u32[]{:S(2)}) collective-permute-start(f32[256,256]{1,0:T(8,128)S(1)} %fusion.61), channel_id=1, source_target_pairs={{4,0},{5,1},{6,2},{7,3},{8,4},{9,5},{10,6},{11,7},{12,8},{13,9},{1... | collective-permute-start | bytes 786440 | tf_op jit(solution)/shard_map/ppermute | solution.py:199
  320.6 159.0 %collective-permute-start.10 = (f32[256]{0:T(256)S(1)}, f32[256]{0:T(256)S(1)}, u32[]{:S(2)}, u32[]{:S(2)}) collective-permute-start(f32[256]{0:T(256)S(1)} %add.197), channel_id=1, source_target_pairs={{8,0},{9,1},{10,2},{11,3},{12,4},{13,5},{14,6},{15,7},{24,16},{25,... | collective-permute-start | bytes 3080 | tf_op jit(solution)/shard_map/ppermute | solution.py:199
  330.2 167.3 %collective-permute-start.14 = (f32[256,256]{1,0:T(8,128)S(1)}, f32[256,256]{1,0:T(8,128)S(1)}, u32[]{:S(2)}, u32[]{:S(2)}) collective-permute-start(f32[256,256]{1,0:T(8,128)S(1)} %convolution_add_fusion.1), channel_id=1, source_target_pairs={{8,0},{9,1},{10,2},{11,3},{12,4},{13,5},{14,6},{15,7},{24,16},{25,... | collective-permute-start | bytes 786440 | tf_op jit(solution)/shard_map/ppermute | solution.py:199
